TPU v7x, 128 devices: a whole 4x4x4 slice. The times are simulated.
128 devices in a mesh: row: 64 (over z, y, x), col: 2 (over core).
Axes of the slice: x: 4, y: 4, z: 4, core: 2. Of those that a mesh axis runs over, the one named last changes fastest.
Arguments:
- rhs: float32 [2, 64, 1024, 1024], P(None, 'row', None, 'col'), may hold values from -8 to 8
- panels: float32 [2, 2, 64, 1024, 1024], P(None, None, 'row', None, 'col'), may hold values from -0.1875 to 0.1875
- inverses: float32 [2, 1024, 1024], replicated, may hold values from -1 to 4, as said below
Outputs:
- result: float32 [2, 64, 1024, 1024], P(None, 'row', None, 'col')
Inputs may be any that keep to these rules, and one draw needn't show every extreme that they name: Each inverses[k] is lower triangular with a positive diagonal.
All inputs are finite; a program needn't handle non-finite values.
Results may differ from a plain program's by a relative error of at most 0.000075.
Values sent between devices are 32-bit elements; how exact they have to be, the bound alone decides.
No kernel may reach another device: no remote copies, remote signals or barrier semaphores. Data moves between devices by JAX's collectives and lax.ppermute only.
A program may use at most 128 MiB of HBM per device.

v0:
```python
import jax
import jax.numpy as jnp
from jax import lax
from jax.sharding import PartitionSpec as P


def per_device(rhs, panels, inverses):
    highest = lax.Precision.HIGH
    high = highest
    row_index = lax.axis_index("row")
    row_count = lax.axis_size("row")
    col_index = lax.axis_index("col")
    slot_count = rhs.shape[0]
    half = panels.shape[-1]
    block_ids = (jnp.arange(slot_count, dtype=jnp.int32) * row_count + row_index)[
        :, None, None, None
    ]
    swap = [(0, 1), (1, 0)]

    def dot(a, b):
        return jnp.dot(a, b, precision=highest, preferred_element_type=jnp.float32)

    other_panels = lax.ppermute(panels, "col", swap)

    def kept_at(owner, value):
        return jnp.where(row_index == owner, value, 0).astype(value.dtype)

    spread = lax.psum((kept_at(0, rhs[0, 0]), kept_at(1, rhs[0, 0]), kept_at(1, panels[0, 0, 0])), "row")

    def rows_of(solved, which):
        return lax.dynamic_slice_in_dim(solved, which * half, half, axis=0)

    def split_product(mine, other, solved, spec, precision):
        a = jnp.einsum(spec, mine, rows_of(solved, col_index), precision=precision,
                       preferred_element_type=jnp.float32)
        b = jnp.einsum(spec, other, rows_of(solved, 1 - col_index), precision=precision,
                       preferred_element_type=jnp.float32)
        return a + b

    high = highest

    whole = jnp.where(
        col_index == 0,
        jnp.concatenate([panels, other_panels], axis=-1),
        jnp.concatenate([other_panels, panels], axis=-1),
    )

    def full_product(tiles, right):
        return jnp.einsum("sqin,nm->sqim", tiles, right, precision=high,
                          preferred_element_type=jnp.float32)

    first = full_product(whole[0], inverses[0])
    second = full_product(whole[1], inverses[1])
    is_row0 = block_ids == 0
    is_row1 = block_ids == 1
    zero = jnp.zeros_like(first)
    first = jnp.where(is_row0, -inverses[0], jnp.where(is_row1, zero, first))
    second = jnp.where(is_row0, zero, jnp.where(is_row1, -inverses[1], second))
    kept = jnp.where(block_ids >= 2, rhs, 0).astype(rhs.dtype)
    first = jnp.concatenate([first.reshape((-1,) + first.shape[-2:]), inverses[0][None]])
    spread, first, second, kept = lax.optimization_barrier((spread, first, second, kept))
    rhs0, rhs1, tile_mine = spread[0], spread[1], spread[2]
    tile_other = lax.ppermute(tile_mine, "col", swap)

    firsts = jnp.einsum("kim,mr->kir", first, rhs0, precision=high,
                        preferred_element_type=jnp.float32)
    solved0 = firsts[-1]
    sectioned1 = rhs1 - split_product(tile_mine, tile_other, solved0, "in,nr->ir", highest)
    sectioned1 = lax.optimization_barrier(sectioned1)
    apply = "sqim,mr->sqir"
    out = kept - firsts[:-1].reshape(kept.shape)
    return out - jnp.einsum(apply, second, sectioned1, precision=high,
                            preferred_element_type=jnp.float32)


def solution(mesh):
    placed = (P(None, "row", None, "col"), P(None, None, "row", None, "col"), P())
    return jax.shard_map(
        per_device,
        mesh=mesh,
        in_specs=placed,
        out_specs=P(None, "row", None, "col"),
        check_vma=False,
    )
```

profile of v0, /device:TPU:1, one launch (start us, length us, event | category | flops | bytes accessed | tf_op | source)
XLA Modules:
  0.0 201.8 jit_solution(2811658169054325667)
XLA Ops:
  6.5 0.0 all-reduce.3.cloned.1.call-start
  6.5 1.4 collective-permute-start
  8.0 0.0 copy-start.2
  8.0 3.4 %select_bitcast_fusion.1 = f32[1024,512]{1,0:T(8,128)} fusion(f32[2,2,1,1024,512]{4,3,2,1,0:T(8,128)} %param.4, pred[]{:T(512)S(6)} %eq.27), kind=kLoop, calls=%fused_computation.24 | loop fusion | flops 524288 | bytes 4194305 | tf_op jit(solution)/shard_map/jit(_where)/select_n | solution.py:26
  11.3 0.0 copy-done.2
  11.3 2.5 %select_bitcast_fusion.2 = (f32[1024,512]{1,0:T(8,128)}, f32[1024,512]{1,0:T(8,128)}) fusion(f32[2,1,1024,512]{3,2,1,0:T(8,128)S(1)} %copy-done.2, pred[]{:T(512)S(6)} %eq.27, pred[]{:T(512)S(6)} %eq.26), kind=kLoop, calls=%fused_computation.25 | loop fusion | flops 1048576 | bytes 6291458 | tf_op jit(solution)/shard_map/jit(_where)/select_n | solution.py:26
  13.8 0.0 all-reduce.3.cloned.1.call-update
  13.8 0.0 copy-start.3
  13.8 0.0 slice-start
  13.9 0.0 slice-start.1
  13.9 2.1 %copy-done.3 = f32[2,1,1024,512]{3,2,1,0:T(8,128)S(1)} copy-done((f32[2,1,1024,512]{3,2,1,0:T(8,128)S(1)}, f32[2,1,1024,512]{3,2,1,0:T(8,128)}, u32[]{:S(2)}) %copy-start.3) | copy-done | bytes 4194328
  16.0 2.7 %bitcast_select_fusion = f32[2,1,1024,512]{3,2,0,1:T(8,128)} fusion(f32[2,1,1024,512]{3,2,1,0:T(8,128)S(1)} %copy-done.3, pred[2]{0:T(512)(128)(4,1)S(1)} %get-tuple-element.24), kind=kLoop, calls=%fused_computation.14 | loop fusion | flops 1048576 | bytes 8388610 | tf_op jit(solution)/shard_map/jit(_where)/select_n | solution.py:59
  18.8 0.0 slice-done
  18.8 1.2 slice-done.1
  20.0 4.3 %bitcast_negate_fusion = (f32[1024,1024]{1,0:T(8,128)}, f32[1024,1024]{1,0:T(8,128)}) fusion(f32[2,1024,1024]{2,1,0:T(8,128)S(1)} %bitcast.68), kind=kLoop, calls=%fused_computation.16 | loop fusion | flops 2097152 | bytes 16777216 | tf_op jit(solution)/shard_map/neg | solution.py:58
  24.3 0.0 collective-permute-done
  24.3 14.8 %maximum_select_fusion = f32[2,2,1,1024,1024]{4,3,1,2,0:T(8,128)S(1)} fusion(f32[2,2,1,1024,512]{4,3,1,2,0:T(8,128)} %collective-permute-done, f32[2,2,1,1024,512]{4,3,1,2,0:T(8,128)} %bitcast.72, pred[]{:T(512)S(6)} %eq.30), kind=kLoop, calls=%fused_computation | loop fusion | flops 12582912 | bytes 33554432 | tf_op jit(solution)/shard_map/jit(_where)/select_n | solution.py:42
  39.1 0.0 copy-start
  39.1 6.1 %copy-done = f32[2,2,1,1024,1024]{4,3,1,2,0:T(8,128)} copy-done((f32[2,2,1,1024,1024]{4,3,1,2,0:T(8,128)}, f32[2,2,1,1024,1024]{4,3,1,2,0:T(8,128)S(1)}, u32[]{:S(2)}) %copy-start) | copy-done | bytes 16777240
  45.2 0.0 slice-start.2
  45.2 18.3 %select_select_fusion = f32[2,1024,1024]{2,1,0:T(8,128)} fusion(f32[1024,1024]{1,0:T(8,128)} %get-tuple-element.21, pred[2]{0:T(512)(128)(4,1)S(1)} %get-tuple-element.25, pred[2]{0:T(512)(128)(4,1)S(1)} %broadcast_compare_fusion.2, f32[2,2,1,1024,1024]{4,3,1,2,0:T(8,128)S(1)} %maximum_select_fusion, f32[2,1024,1024]{2,1,0:T(8,128)} %param.5), kind=kOutput, calls=%fused_computation.9 | convolution fusion | flops 12889096192 | bytes 25166848 | tf_op jit(solution)/shard_map/sqin,nm->sqim/dot_general | solution.py:49
  63.5 0.0 slice-done.2
  63.5 10.2 %pad_maximum_fusion = f32[3,1024,1024]{2,1,0:T(8,128)} fusion(f32[1,1024,1024]{2,1,0:T(8,128)S(1)} %slice-done.2, f32[2,1024,1024]{2,1,0:T(8,128)} %select_select_fusion), kind=kLoop, calls=%fused_computation.1 | loop fusion | flops 3145728 | bytes 25165824 | tf_op jit(solution)/shard_map/concatenate | solution.py:60
  73.7 19.1 %select_bitcast_fusion = f32[2,1,1024,1024]{3,2,0,1:T(8,128)} fusion(f32[1024,1024]{1,0:T(8,128)} %get-tuple-element.20, pred[2]{0:T(512)(128)(4,1)S(1)} %get-tuple-element.25, pred[2]{0:T(512)(128)(4,1)S(1)} %broadcast_compare_fusion.2, f32[2,1024,1024]{2,1,0:T(8,128)} %param.5, f32[2,2,1,1024,1024]{4,3,1,2,0:T(8,128)} %copy-done), kind=kOutput, calls=%fused_computation.8 | convolution fusion | flops 12889096192 | bytes 25165828 | tf_op jit(solution)/shard_map/sqin,nm->sqim/dot_general | solution.py:49
  92.8 70.9 %all-reduce.3.cloned.1.call-done = (f32[1024,512]{1,0:T(8,128)}, f32[1024,512]{1,0:T(8,128)}, f32[1024,512]{1,0:T(8,128)}) async-done(((f32[1024,512]{1,0:T(8,128)}, f32[1024,512]{1,0:T(8,128)}, f32[1024,512]{1,0:T(8,128)}), (f32[1024,512]{1,0:T(8,128)}, f32[1024,512]{1,0:T(8,128)}, f32[1024,512]{1,0:T(8,128)})) %all-reduce.3.cloned.1.call-update) | async-done | bytes 6291472 | tf_op jit(solution)/shard_map/psum | solution.py:28
  163.7 1.0 collective-permute-start.1
  164.7 13.5 %fusion.15 = f32[3,1024,512]{2,1,0:T(8,128)S(1)} fusion(f32[3,1024,1024]{2,1,0:T(8,128)} %pad_maximum_fusion, f32[1024,512]{1,0:T(8,128)} %get-tuple-element.13), kind=kOutput, calls=%fused_computation.21 | convolution fusion | flops 9663676416 | bytes 20971520 | tf_op jit(solution)/shard_map/kim,mr->kir/dot_general | solution.py:65
  178.2 0.0 copy-start.4
  178.2 0.2 slice.39
  178.4 1.4 copy-done.4
  179.8 0.0 copy-start.5
  179.8 0.0 slice-start.3
  179.8 1.8 fusion.19
  181.6 0.0 slice-start.4
  181.6 0.0 collective-permute-done.1
  181.6 1.8 fusion.17
  183.4 0.0 copy-done.5
  183.5 0.8 add_subtract_fusion
  184.2 0.0 slice-done.3
  184.2 0.0 slice-done.4
  184.3 0.0 copy-start.1
  184.3 7.1 %fusion.2 = f32[2,1024,512]{2,1,0:T(8,128)S(1)} fusion(f32[2,1,1024,1024]{3,2,0,1:T(8,128)S(1)} %bitcast.70, f32[1024,512]{1,0:T(8,128)S(1)} %add_subtract_fusion), kind=kOutput, calls=%fused_computation.6 | convolution fusion | flops 6442450944 | bytes 14680064 | tf_op jit(solution)/shard_map/sqim,mr->sqir/dot_general | solution.py:72
  191.4 0.0 copy-done.1
  191.4 3.6 %fusion.6 = f32[2,1,1024,512]{3,2,1,0:T(8,128)} fusion(f32[2,1,1024,512]{3,2,0,1:T(8,128)S(1)} %copy-done.1, f32[3,1024,512]{2,1,0:T(8,128)S(1)} %fusion.15, f32[2,1024,512]{2,1,0:T(8,128)S(1)} %fusion.2), kind=kLoop, calls=%fused_computation.13 | loop fusion | flops 2097152 | bytes 16777216 | tf_op jit(solution)/shard_map/sub | solution.py:72
  (4 shorter events, 0.0 us)
Async XLA Ops:
  6.5 157.2 %all-reduce.3.cloned.1.call-start = ((), (), s32[]{:S(2)}) async-start(), calls=%async_computation | async-start | bytes 12582912 | tf_op jit(solution)/shard_map/psum | solution.py:28
  6.5 17.8 %collective-permute-start = (f32[2,2,1,1024,512]{4,3,1,2,0:T(8,128)}, f32[2,2,1,1024,512]{4,3,1,2,0:T(8,128)}, u32[]{:S(2)}, u32[]{:S(2)}) collective-permute-start(f32[2,2,1,1024,512]{4,3,1,2,0:T(8,128)} %bitcast.71), channel_id=1, source_target_pairs={{0,1},{1,0},{2,3},{3,2},{4,5},{5,4},{6,7},{7,6},{8,9},{9,8},{10,11... | collective-permute-start | bytes 25165832 | tf_op jit(solution)/shard_map/ppermute | solution.py:23
  8.0 3.4 %copy-start.2 = (f32[2,1,1024,512]{3,2,1,0:T(8,128)S(1)}, f32[2,1,1024,512]{3,2,1,0:T(8,128)}, u32[]{:S(2)}) copy-start(f32[2,1,1024,512]{3,2,1,0:T(8,128)} %param.3) | copy-start | bytes 12582916
  13.8 2.2 %copy-start.3 = (f32[2,1,1024,512]{3,2,1,0:T(8,128)S(1)}, f32[2,1,1024,512]{3,2,1,0:T(8,128)}, u32[]{:S(2)}) copy-start(f32[2,1,1024,512]{3,2,1,0:T(8,128)} %param.3) | copy-start | bytes 12582916
  13.8 4.9 %slice-start = ((s8[8388608]{0:T(1024)(128)(4,1)}), s8[4194304]{0:T(1024)(128)(4,1)S(1)}, s32[]{:S(2)}) async-start(s8[8388608]{0:T(1024)(128)(4,1)} %bitcast.67), calls=%async_computation.1 | async-start | bytes 8388608
  13.9 6.1 %slice-start.1 = ((s8[8388608]{0:T(1024)(128)(4,1)}), s8[4194304]{0:T(1024)(128)(4,1)S(1)}, s32[]{:S(2)}) async-start(s8[8388608]{0:T(1024)(128)(4,1)} %bitcast.67), calls=%async_computation.2 | async-start | bytes 8388608
  39.1 6.1 %copy-start = (f32[2,2,1,1024,1024]{4,3,1,2,0:T(8,128)}, f32[2,2,1,1024,1024]{4,3,1,2,0:T(8,128)S(1)}, u32[]{:S(2)}) copy-start(f32[2,2,1,1024,1024]{4,3,1,2,0:T(8,128)S(1)} %maximum_select_fusion) | copy-start | bytes 50331652
  45.2 18.3 %slice-start.2 = ((f32[2,1024,1024]{2,1,0:T(8,128)}), f32[1,1024,1024]{2,1,0:T(8,128)S(1)}, s32[]{:S(2)}) async-start(f32[2,1024,1024]{2,1,0:T(8,128)} %param.5), calls=%async_computation.3 | async-start | bytes 8388608 | tf_op jit(solution)/shard_map/slice | solution.py:57
  163.7 17.9 %collective-permute-start.1 = (f32[1024,512]{1,0:T(8,128)}, f32[1024,512]{1,0:T(8,128)S(1)}, u32[]{:S(2)}, u32[]{:S(2)}) collective-permute-start(f32[1024,512]{1,0:T(8,128)} %get-tuple-element.16), channel_id=1, source_target_pairs={{0,1},{1,0},{2,3},{3,2},{4,5},{5,4},{6,7},{7,6},{8,9},{9,8},{10,11... | collective-permute-start | bytes 6291464 | tf_op jit(solution)/shard_map/ppermute | solution.py:63
  178.2 1.6 copy-start.4
  179.8 3.7 %copy-start.5 = (f32[1024,512]{1,0:T(8,128)S(1)}, f32[1024,512]{1,0:T(8,128)}, u32[]{:S(2)}) copy-start(f32[1024,512]{1,0:T(8,128)} %get-tuple-element.15) | copy-start | bytes 6291460
  179.8 4.5 %slice-start.3 = ((s8[8388608]{0:T(1024)(128)(4,1)}), s8[4194304]{0:T(1024)(128)(4,1)S(1)}, s32[]{:S(2)}) async-start(s8[8388608]{0:T(1024)(128)(4,1)} %bitcast.69), calls=%async_computation.4 | async-start | bytes 8388608
  181.6 2.6 %slice-start.4 = ((s8[8388608]{0:T(1024)(128)(4,1)}), s8[4194304]{0:T(1024)(128)(4,1)S(1)}, s32[]{:S(2)}) async-start(s8[8388608]{0:T(1024)(128)(4,1)} %bitcast.69), calls=%async_computation.5 | async-start | bytes 8388608
  184.3 7.1 %copy-start.1 = (f32[2,1,1024,512]{3,2,0,1:T(8,128)S(1)}, f32[2,1,1024,512]{3,2,0,1:T(8,128)}, u32[]{:S(2)}) copy-start(f32[2,1,1024,512]{3,2,0,1:T(8,128)} %bitcast_select_fusion) | copy-start | bytes 12582916
Sparse Core Ops, SparseCore 0:
  13.9 149.6 all-reduce.2
where the time goes:
time: 202 us
  waiting for transfers between devices  70.9 us (35%)
  matrix products  61.7 us (31%)
  other arithmetic  42.2 us (21%)
  between operations  13.6 us (7%)
  local copies, waits for them, and re-layouts  11.1 us (5%)
  starting transfers between devices  2.41 us (1%)
    psum x1, waiting for transfers between devices, per_device(): lax.psum((kept_at(0, rhs[0, 0]), kept_at(1, rhs[0, 0]), kept_at(1, panels...  70.9 us
    dot_general x2, matrix products, full_product(): jnp.einsum('sqin,nm->sqim', tiles, right, precision=high, preferred_eleme...  37.4 us
    select_n x1, other arithmetic, per_device(): jnp.where(col_index == 0, jnp.concatenate([panels, other_panels], axis=-1...  14.8 us
    dot_general x1, matrix products, per_device(): jnp.einsum('kim,mr->kir', first, rhs0, precision=high, preferred_element_...  13.5 us
    unnamed x20, local copies, waits for them, and re-layouts  10.9 us
    concatenate x1, other arithmetic, per_device(): jnp.concatenate([first.reshape((-1,) + first.shape[-2:]), inverses[0][Non...  10.2 us
    dot_general x1, matrix products, per_device(): jnp.einsum(apply, second, sectioned1, precision=high, preferred_element_t...  7.12 us
    select_n x2, other arithmetic, kept_at(): return jnp.where(row_index == owner, value, 0).astype(value.dtype)  5.84 us
  transfers between devices with their start and end apart: 3, of which 1 were waited for; matrix products, arithmetic and copies ran while one was open for 45% of the time, Pallas kernels for 0%

commit v1 on v0

--- a/solution.py
+++ b/solution.py
@@ -27,37 +27,27 @@
 
     spread = lax.psum((kept_at(0, rhs[0, 0]), kept_at(1, rhs[0, 0]), kept_at(1, panels[0, 0, 0])), "row")
 
-    def rows_of(solved, which):
-        return lax.dynamic_slice_in_dim(solved, which * half, half, axis=0)
 
-    def split_product(mine, other, solved, spec, precision):
-        a = jnp.einsum(spec, mine, rows_of(solved, col_index), precision=precision,
-                       preferred_element_type=jnp.float32)
-        b = jnp.einsum(spec, other, rows_of(solved, 1 - col_index), precision=precision,
-                       preferred_element_type=jnp.float32)
-        return a + b
+    whole = jnp.concatenate([panels, other_panels], axis=-1)
 
-    high = highest
+    def mine_first(matrix):
+        return jnp.roll(matrix, -col_index * half, axis=0)
 
-    whole = jnp.where(
-        col_index == 0,
-        jnp.concatenate([panels, other_panels], axis=-1),
-        jnp.concatenate([other_panels, panels], axis=-1),
-    )
+    inverse0, inverse1 = mine_first(inverses[0]), mine_first(inverses[1])
 
     def full_product(tiles, right):
         return jnp.einsum("sqin,nm->sqim", tiles, right, precision=high,
                           preferred_element_type=jnp.float32)
 
-    first = full_product(whole[0], inverses[0])
-    second = full_product(whole[1], inverses[1])
+    first = full_product(whole[0], inverse0)
+    second = full_product(whole[1], inverse1)
     is_row0 = block_ids == 0
     is_row1 = block_ids == 1
     zero = jnp.zeros_like(first)
     first = jnp.where(is_row0, -inverses[0], jnp.where(is_row1, zero, first))
     second = jnp.where(is_row0, zero, jnp.where(is_row1, -inverses[1], second))
     kept = jnp.where(block_ids >= 2, rhs, 0).astype(rhs.dtype)
-    first = jnp.concatenate([first.reshape((-1,) + first.shape[-2:]), inverses[0][None]])
+    first = jnp.concatenate([first.reshape((-1,) + first.shape[-2:]), inverse0[None]])
     spread, first, second, kept = lax.optimization_barrier((spread, first, second, kept))
     rhs0, rhs1, tile_mine = spread[0], spread[1], spread[2]
     tile_other = lax.ppermute(tile_mine, "col", swap)
@@ -65,7 +55,7 @@
     firsts = jnp.einsum("kim,mr->kir", first, rhs0, precision=high,
                         preferred_element_type=jnp.float32)
     solved0 = firsts[-1]
-    sectioned1 = rhs1 - split_product(tile_mine, tile_other, solved0, "in,nr->ir", highest)
+    sectioned1 = rhs1 - dot(jnp.concatenate([tile_mine, tile_other], axis=-1), solved0)
     sectioned1 = lax.optimization_barrier(sectioned1)
     apply = "sqim,mr->sqir"
     out = kept - firsts[:-1].reshape(kept.shape)

time: 202 us -> 200 us (0.990)
  waiting for transfers between devices: 70.9 us -> 84.4 us
  other arithmetic: 42.2 us -> 29.4 us
  local copies, waits for them, and re-layouts: 11.1 us -> 8.4 us
    select_n x1 -> x0, other arithmetic: 14.8 us -> none  [per_device(): jnp.where(col_index == 0, jnp.concatenate([panels, other_panels], axis=-1...]
    psum x1, waiting for transfers between devices: 70.9 us -> 84.4 us  [per_device(): lax.psum((kept_at(0, rhs[0, 0]), kept_at(1, rhs[0, 0]), kept_at(1, panels...]
    unnamed x20 -> x16, local copies, waits for them, and re-layouts: 10.9 us -> 1.72 us
    squeeze x0 -> x1, local copies, waits for them, and re-layouts: none -> 6.67 us  [per_device(): second = jnp.where(is_row0, zero, jnp.where(is_row1, -inverses[1], second))]
  transfers between devices with their start and end apart: 3 -> 3, of which waited for: 1 -> 1; matrix products, arithmetic and copies ran while one was open for 45% -> 42% of each run, Pallas kernels for 0% -> 0%
where the time goes in v1:
time: 200 us
  waiting for transfers between devices  84.4 us (42%)
  matrix products  61.9 us (31%)
  other arithmetic  29.4 us (15%)
  between operations  13.5 us (7%)
  local copies, waits for them, and re-layouts  8.4 us (4%)
  starting transfers between devices  2.41 us (1%)
    psum x1, waiting for transfers between devices, per_device(): lax.psum((kept_at(0, rhs[0, 0]), kept_at(1, rhs[0, 0]), kept_at(1, panels...  84.4 us
    dot_general x2, matrix products, full_product(): jnp.einsum('sqin,nm->sqim', tiles, right, precision=high, preferred_eleme...  37.7 us
    dot_general x1, matrix products, per_device(): jnp.einsum('kim,mr->kir', first, rhs0, precision=high, preferred_element_...  13.5 us
    concatenate x1, other arithmetic, per_device(): jnp.concatenate([first.reshape((-1,) + first.shape[-2:]), inverse0[None]])  10.2 us
    dot_general x1, matrix products, per_device(): jnp.einsum(apply, second, sectioned1, precision=high, preferred_element_t...  7.12 us
    squeeze x1, local copies, waits for them, and re-layouts, per_device(): second = jnp.where(is_row0, zero, jnp.where(is_row1, -inverses[1], second))  6.67 us
    select_n x2, other arithmetic, kept_at(): return jnp.where(row_index == owner, value, 0).astype(value.dtype)  5.94 us
    neg x1, other arithmetic, per_device(): second = jnp.where(is_row0, zero, jnp.where(is_row1, -inverses[1], second))  4.34 us
  transfers between devices with their start and end apart: 3, of which 1 were waited for; matrix products, arithmetic and copies ran while one was open for 42% of the time, Pallas kernels for 0%

profile of v1, /device:TPU:1, one launch (start us, length us, event | category | flops | bytes accessed | tf_op | source)
XLA Modules:
  0.0 200.0 jit_solution(16188594010539345716)
XLA Ops:
  6.5 0.0 all-reduce.3.cloned.1.call-start
  6.5 1.4 collective-permute-start
  8.0 0.0 copy-start.1
  8.0 3.3 %select_bitcast_fusion.1 = f32[1024,512]{1,0:T(8,128)} fusion(f32[2,2,1,1024,512]{4,3,2,1,0:T(8,128)} %param.6, pred[]{:T(512)S(6)} %eq.26), kind=kLoop, calls=%fused_computation.37 | loop fusion | flops 524288 | bytes 4194305 | tf_op jit(solution)/shard_map/jit(_where)/select_n | solution.py:26
  11.3 0.0 copy-done.1
  11.3 2.6 %select_bitcast_fusion.2 = (f32[1024,512]{1,0:T(8,128)}, f32[1024,512]{1,0:T(8,128)}) fusion(f32[2,1,1024,512]{3,2,1,0:T(8,128)S(1)} %copy-done.1, pred[]{:T(512)S(6)} %eq.26, pred[]{:T(512)S(6)} %eq.25), kind=kLoop, calls=%fused_computation.38 | loop fusion | flops 1048576 | bytes 6291458 | tf_op jit(solution)/shard_map/jit(_where)/select_n | solution.py:26
  13.9 0.0 all-reduce.3.cloned.1.call-update
  14.0 6.7 %slice_bitcast_fusion.1 = (f32[1024,1024]{1,0:T(8,128)}, f32[1024,1024]{1,0:T(8,128)S(1)}) fusion(f32[2,1024,1024]{2,1,0:T(8,128)} %param.7), kind=kLoop, calls=%fused_computation.31 | loop fusion | bytes 16777216 | tf_op jit(solution)/shard_map/squeeze | solution.py:48
  20.7 0.0 copy-start.2
  20.7 0.0 slice-start
  20.7 2.0 fusion.34
  22.7 0.0 slice-start.1
  22.7 0.2 copy-done.2
  22.8 2.8 %bitcast_select_fusion = f32[2,1,1024,512]{3,2,0,1:T(8,128)} fusion(f32[2,1,1024,512]{3,2,1,0:T(8,128)S(1)} %copy-done.2, pred[2]{0:T(512)(128)(4,1)S(1)} %get-tuple-element.27), kind=kLoop, calls=%fused_computation.29 | loop fusion | flops 1048576 | bytes 8388610 | tf_op jit(solution)/shard_map/jit(_where)/select_n | solution.py:49
  25.7 0.0 slice-done
  25.7 1.5 slice-done.1
  27.2 4.3 %fusion.41 = (f32[1024,1024]{1,0:T(8,128)}, f32[1024,1024]{1,0:T(8,128)}) fusion(f32[2,1024,1024]{2,1,0:T(8,128)S(1)} %bitcast.68), kind=kLoop, calls=%fused_computation.51 | loop fusion | flops 2097152 | bytes 16777216 | tf_op jit(solution)/shard_map/neg | solution.py:48
  31.6 0.0 collective-permute-done
  31.6 18.4 %select_select_fusion = f32[2,1024,1024]{2,1,0:T(8,128)} fusion(f32[1024,1024]{1,0:T(8,128)} %get-tuple-element.24, pred[2]{0:T(512)(128)(4,1)S(1)} %get-tuple-element.28, pred[2]{0:T(512)(128)(4,1)S(1)} %broadcast_compare_fusion.2, f32[2,2,1,1024,512]{4,3,1,2,0:T(8,128)} %bitcast.70, f32[2,2,1,1024,512]{4,3,1,2,0:T(8,128)} %collective-permute-done, ...), kind=kOutput, calls=%fused_computation.17 | convolution fusion | flops 12892241920 | bytes 33554440 | tf_op jit(solution)/shard_map/sqin,nm->sqim/dot_general | solution.py:39
  50.0 10.2 %pad_maximum_fusion = f32[3,1024,1024]{2,1,0:T(8,128)} fusion(f32[1,1024,1024]{2,1,0:T(8,128)S(1)} %fusion.34, f32[2,1024,1024]{2,1,0:T(8,128)} %select_select_fusion), kind=kLoop, calls=%fused_computation.2 | loop fusion | flops 3145728 | bytes 25165824 | tf_op jit(solution)/shard_map/concatenate | solution.py:50
  60.2 19.3 %select_bitcast_fusion = f32[2,1,1024,1024]{3,2,0,1:T(8,128)} fusion(f32[1024,1024]{1,0:T(8,128)} %get-tuple-element.23, pred[2]{0:T(512)(128)(4,1)S(1)} %get-tuple-element.28, pred[2]{0:T(512)(128)(4,1)S(1)} %broadcast_compare_fusion.2, s32[]{:T(128)S(6)} %select_n.81, f32[1024,1024]{1,0:T(8,128)} %get-tuple-element.21, ...), kind=kOutput, calls=%fused_computation.16 | convolution fusion | flops 12892241920 | bytes 33554440 | tf_op jit(solution)/shard_map/sqin,nm->sqim/dot_general | solution.py:39
  79.5 84.4 %all-reduce.3.cloned.1.call-done = (f32[1024,512]{1,0:T(8,128)}, f32[1024,512]{1,0:T(8,128)}, f32[1024,512]{1,0:T(8,128)}) async-done(((f32[1024,512]{1,0:T(8,128)}, f32[1024,512]{1,0:T(8,128)}, f32[1024,512]{1,0:T(8,128)}), (f32[1024,512]{1,0:T(8,128)}, f32[1024,512]{1,0:T(8,128)}, f32[1024,512]{1,0:T(8,128)})) %all-reduce.3.cloned.1.call-update) | async-done | bytes 6291472 | tf_op jit(solution)/shard_map/psum | solution.py:28
  163.8 0.0 copy-start.5
  163.8 1.0 collective-permute-start.1
  164.8 13.5 %fusion.31 = f32[3,1024,512]{2,1,0:T(8,128)S(1)} fusion(f32[3,1024,1024]{2,1,0:T(8,128)} %pad_maximum_fusion, f32[1024,512]{1,0:T(8,128)} %get-tuple-element.14), kind=kOutput, calls=%fused_computation.35 | convolution fusion | flops 9663676416 | bytes 20971520 | tf_op jit(solution)/shard_map/kim,mr->kir/dot_general | solution.py:55
  178.3 0.0 copy-start.4
  178.3 0.0 collective-permute-done.1
  178.3 0.0 copy-done.5
  178.3 0.0 copy-start.3
  178.3 3.5 %fusion.17 = f32[1024,512]{1,0:T(8,128)S(1)} fusion(f32[1024,512]{1,0:T(8,128)S(1)} %collective-permute-done.1, f32[1024,512]{1,0:T(8,128)S(1)} %copy-done.5, f32[3,1024,512]{2,1,0:T(8,128)S(1)} %fusion.31), kind=kOutput, calls=%fused_computation.25 | convolution fusion | flops 3222274048 | bytes 8388608 | tf_op jit(solution)/shard_map/dot_general | solution.py:21
  181.9 0.0 copy-done.4
  181.9 0.5 sub.13
  182.4 0.0 copy-done.3
  182.4 0.0 copy-start
  182.4 7.1 %fusion.8 = f32[2,1024,512]{2,1,0:T(8,128)S(1)} fusion(f32[2,1,1024,1024]{3,2,0,1:T(8,128)S(1)} %copy-done.3, f32[1024,512]{1,0:T(8,128)S(1)} %sub.13), kind=kOutput, calls=%fused_computation.14 | convolution fusion | flops 6442450944 | bytes 14680064 | tf_op jit(solution)/shard_map/sqim,mr->sqir/dot_general | solution.py:62
  189.5 0.0 copy-done
  189.5 3.6 %fusion.16 = f32[2,1,1024,512]{3,2,1,0:T(8,128)} fusion(f32[2,1,1024,512]{3,2,0,1:T(8,128)S(1)} %copy-done, f32[3,1024,512]{2,1,0:T(8,128)S(1)} %fusion.31, f32[2,1024,512]{2,1,0:T(8,128)S(1)} %fusion.8), kind=kLoop, calls=%fused_computation.24 | loop fusion | flops 2097152 | bytes 16777216 | tf_op jit(solution)/shard_map/sub | solution.py:62
  (3 shorter events, 0.0 us)
Async XLA Ops:
  6.5 157.3 %all-reduce.3.cloned.1.call-start = ((), (), s32[]{:S(2)}) async-start(), calls=%async_computation | async-start | bytes 12582912 | tf_op jit(solution)/shard_map/psum | solution.py:28
  6.5 25.0 %collective-permute-start = (f32[2,2,1,1024,512]{4,3,1,2,0:T(8,128)}, f32[2,2,1,1024,512]{4,3,1,2,0:T(8,128)}, u32[]{:S(2)}, u32[]{:S(2)}) collective-permute-start(f32[2,2,1,1024,512]{4,3,1,2,0:T(8,128)} %bitcast.69), channel_id=1, source_target_pairs={{0,1},{1,0},{2,3},{3,2},{4,5},{5,4},{6,7},{7,6},{8,9},{9,8},{10,11... | collective-permute-start | bytes 25165832 | tf_op jit(solution)/shard_map/ppermute | solution.py:23
  8.0 3.3 %copy-start.1 = (f32[2,1,1024,512]{3,2,1,0:T(8,128)S(1)}, f32[2,1,1024,512]{3,2,1,0:T(8,128)}, u32[]{:S(2)}) copy-start(f32[2,1,1024,512]{3,2,1,0:T(8,128)} %param.5) | copy-start | bytes 12582916
  20.7 2.2 %copy-start.2 = (f32[2,1,1024,512]{3,2,1,0:T(8,128)S(1)}, f32[2,1,1024,512]{3,2,1,0:T(8,128)}, u32[]{:S(2)}) copy-start(f32[2,1,1024,512]{3,2,1,0:T(8,128)} %param.5) | copy-start | bytes 12582916
  20.7 5.0 %slice-start = ((s8[8388608]{0:T(1024)(128)(4,1)}), s8[4194304]{0:T(1024)(128)(4,1)S(1)}, s32[]{:S(2)}) async-start(s8[8388608]{0:T(1024)(128)(4,1)} %bitcast.67), calls=%async_computation.1 | async-start | bytes 8388608
  22.7 4.6 %slice-start.1 = ((s8[8388608]{0:T(1024)(128)(4,1)}), s8[4194304]{0:T(1024)(128)(4,1)S(1)}, s32[]{:S(2)}) async-start(s8[8388608]{0:T(1024)(128)(4,1)} %bitcast.67), calls=%async_computation.2 | async-start | bytes 8388608
  163.8 14.5 %copy-start.5 = (f32[1024,512]{1,0:T(8,128)S(1)}, f32[1024,512]{1,0:T(8,128)}, u32[]{:S(2)}) copy-start(f32[1024,512]{1,0:T(8,128)} %get-tuple-element.17) | copy-start | bytes 6291460
  163.8 14.5 %collective-permute-start.1 = (f32[1024,512]{1,0:T(8,128)}, f32[1024,512]{1,0:T(8,128)S(1)}, u32[]{:S(2)}, u32[]{:S(2)}) collective-permute-start(f32[1024,512]{1,0:T(8,128)} %get-tuple-element.17), channel_id=1, source_target_pairs={{0,1},{1,0},{2,3},{3,2},{4,5},{5,4},{6,7},{7,6},{8,9},{9,8},{10,11... | collective-permute-start | bytes 6291464 | tf_op jit(solution)/shard_map/ppermute | solution.py:53
  178.3 3.6 %copy-start.4 = (f32[1024,512]{1,0:T(8,128)S(1)}, f32[1024,512]{1,0:T(8,128)}, u32[]{:S(2)}) copy-start(f32[1024,512]{1,0:T(8,128)} %get-tuple-element.16) | copy-start | bytes 6291460
  178.3 4.1 %copy-start.3 = (f32[2,1,1024,1024]{3,2,0,1:T(8,128)S(1)}, f32[2,1,1024,1024]{3,2,0,1:T(8,128)}, u32[]{:S(2)}) copy-start(f32[2,1,1024,1024]{3,2,0,1:T(8,128)} %select_bitcast_fusion) | copy-start | bytes 25165828
  182.4 7.1 %copy-start = (f32[2,1,1024,512]{3,2,0,1:T(8,128)S(1)}, f32[2,1,1024,512]{3,2,0,1:T(8,128)}, u32[]{:S(2)}) copy-start(f32[2,1,1024,512]{3,2,0,1:T(8,128)} %bitcast_select_fusion) | copy-start | bytes 12582916
Sparse Core Ops, SparseCore 0:
  14.1 149.7 all-reduce.2

commit v2 on v1

--- a/solution.py
+++ b/solution.py
@@ -44,21 +44,22 @@
     is_row0 = block_ids == 0
     is_row1 = block_ids == 1
     zero = jnp.zeros_like(first)
-    first = jnp.where(is_row0, -inverses[0], jnp.where(is_row1, zero, first))
+    first = jnp.where(is_row0, inverses[0], jnp.where(is_row1, zero, -first))
     second = jnp.where(is_row0, zero, jnp.where(is_row1, -inverses[1], second))
     kept = jnp.where(block_ids >= 2, rhs, 0).astype(rhs.dtype)
     first = jnp.concatenate([first.reshape((-1,) + first.shape[-2:]), inverse0[None]])
+    kept = jnp.concatenate([kept.reshape((-1,) + kept.shape[-2:]), jnp.zeros_like(kept[0, 0])[None]])
     spread, first, second, kept = lax.optimization_barrier((spread, first, second, kept))
     rhs0, rhs1, tile_mine = spread[0], spread[1], spread[2]
     tile_other = lax.ppermute(tile_mine, "col", swap)
 
-    firsts = jnp.einsum("kim,mr->kir", first, rhs0, precision=high,
-                        preferred_element_type=jnp.float32)
+    firsts = kept + jnp.einsum("kim,mr->kir", first, rhs0, precision=high,
+                               preferred_element_type=jnp.float32)
     solved0 = firsts[-1]
     sectioned1 = rhs1 - dot(jnp.concatenate([tile_mine, tile_other], axis=-1), solved0)
     sectioned1 = lax.optimization_barrier(sectioned1)
     apply = "sqim,mr->sqir"
-    out = kept - firsts[:-1].reshape(kept.shape)
+    out = firsts[:-1].reshape(rhs.shape)
     return out - jnp.einsum(apply, second, sectioned1, precision=high,
                             preferred_element_type=jnp.float32)
 

time: 200 us -> 206 us (1.030)
  waiting for transfers between devices: 84.4 us -> 88.2 us
  matrix products: 61.9 us -> 65.2 us
    add x0 -> x1, other arithmetic: none -> 6.33 us  [per_device(): kept + jnp.einsum('kim,mr->kir', first, rhs0, precision=high, preferred_e...]
    psum x1, waiting for transfers between devices: 84.4 us -> 88.2 us  [per_device(): lax.psum((kept_at(0, rhs[0, 0]), kept_at(1, rhs[0, 0]), kept_at(1, panels...]
    sub x1 -> x0, other arithmetic: 3.57 us -> none  [per_device(): out - jnp.einsum(apply, second, sectioned1, precision=high, preferred_ele...]
    squeeze x1, local copies, waits for them, and re-layouts: 6.67 us -> 3.26 us  [per_device(): second = jnp.where(is_row0, zero, jnp.where(is_row1, -inverses[1], second))]
    concatenate x0 -> x1, local copies, waits for them, and re-layouts: none -> 3.36 us  [per_device(): jnp.concatenate([kept.reshape((-1,) + kept.shape[-2:]), jnp.zeros_like(ke...]
    reshape x0 -> x1, other arithmetic: none -> 2.92 us  [per_device(): kept.reshape((-1,) + kept.shape[-2:])]
    select_n x1 -> x0, other arithmetic: 2.85 us -> none  [per_device(): kept = jnp.where(block_ids >= 2, rhs, 0).astype(rhs.dtype)]
  transfers between devices with their start and end apart: 3 -> 3, of which waited for: 1 -> 1; matrix products, arithmetic and copies ran while one was open for 42% -> 43% of each run, Pallas kernels for 0% -> 0%
where the time goes in v2:
time: 206 us
  waiting for transfers between devices  88.2 us (43%)
  matrix products  65.2 us (32%)
  other arithmetic  30.1 us (15%)
  between operations  13.5 us (7%)
  local copies, waits for them, and re-layouts  6.69 us (3%)
  starting transfers between devices  2.41 us (1%)
    psum x1, waiting for transfers between devices, per_device(): lax.psum((kept_at(0, rhs[0, 0]), kept_at(1, rhs[0, 0]), kept_at(1, panels...  88.2 us
    dot_general x2, matrix products, full_product(): jnp.einsum('sqin,nm->sqim', tiles, right, precision=high, preferred_eleme...  37.4 us
    dot_general x1, matrix products, per_device(): jnp.einsum('kim,mr->kir', first, rhs0, precision=high, preferred_element_...  15.4 us
    concatenate x1, other arithmetic, per_device(): jnp.concatenate([first.reshape((-1,) + first.shape[-2:]), inverse0[None]])  10.2 us
    dot_general x1, matrix products, per_device(): jnp.einsum(apply, second, sectioned1, precision=high, preferred_element_t...  8.77 us
    add x1, other arithmetic, per_device(): kept + jnp.einsum('kim,mr->kir', first, rhs0, precision=high, preferred_e...  6.33 us
    select_n x2, other arithmetic, kept_at(): return jnp.where(row_index == owner, value, 0).astype(value.dtype)  5.76 us
  transfers between devices with their start and end apart: 3, of which 1 were waited for; matrix products, arithmetic and copies ran while one was open for 43% of the time, Pallas kernels for 0%

profile of v2, /device:TPU:1, one launch (start us, length us, event | category | flops | bytes accessed | tf_op | source)
XLA Modules:
  0.0 206.1 jit_solution(220162256675566563)
XLA Ops:
  6.5 0.0 all-reduce.4.cloned.1.call-start
  6.5 1.4 collective-permute-start
  8.0 0.0 copy-start
  8.0 3.3 %select_bitcast_fusion.1 = f32[1024,512]{1,0:T(8,128)} fusion(f32[2,2,1,1024,512]{4,3,2,1,0:T(8,128)} %param.6, pred[]{:T(512)S(6)} %eq.26), kind=kLoop, calls=%fused_computation.36 | loop fusion | flops 524288 | bytes 4194305 | tf_op jit(solution)/shard_map/jit(_where)/select_n | solution.py:26
  11.2 0.0 copy-done
  11.2 2.5 %select_bitcast_fusion.2 = (f32[1024,512]{1,0:T(8,128)}, f32[1024,512]{1,0:T(8,128)}) fusion(f32[2,1,1024,512]{3,2,1,0:T(8,128)S(1)} %copy-done, pred[]{:T(512)S(6)} %eq.26, pred[]{:T(512)S(6)} %eq.25), kind=kLoop, calls=%fused_computation.37 | loop fusion | flops 1048576 | bytes 6291458 | tf_op jit(solution)/shard_map/jit(_where)/select_n | solution.py:26
  13.7 0.0 all-reduce.4.cloned.1.call-update
  13.8 0.0 slice-start
  13.8 2.9 %fusion.19 = f32[2,1024,512]{2,1,0:T(8,128)S(1)} fusion(f32[2,1,1024,512]{3,2,1,0:T(8,128)} %param.5, pred[2]{0:T(512)(128)(4,1)S(1)} %broadcast_compare_fusion), kind=kLoop, calls=%fused_computation.28 | loop fusion | flops 1048576 | bytes 8388610 | tf_op jit(solution)/shard_map/reshape | solution.py:51
  16.7 0.0 slice-start.1
  16.7 3.4 %concatenate.17 = f32[3,1024,512]{2,1,0:T(8,128)} pad(f32[2,1024,512]{2,1,0:T(8,128)S(1)} %fusion.19, f32[]{:T(128)} %constant.36.clone.1), padding=0_1x0_0x0_0 | pad | bytes 10485764 | tf_op jit(solution)/shard_map/concatenate | solution.py:51
  20.1 0.0 slice-done
  20.1 0.0 slice-done.1
  20.2 3.3 %slice_bitcast_fusion = (f32[1024,1024]{1,0:T(8,128)}, f32[1024,1024]{1,0:T(8,128)S(1)}) fusion(f32[2,1024,1024]{2,1,0:T(8,128)S(1)} %bitcast.66), kind=kLoop, calls=%fused_computation.30 | loop fusion | bytes 16777216 | tf_op jit(solution)/shard_map/squeeze | solution.py:48
  23.4 2.0 fusion.37
  25.4 2.4 %fusion.43 = f32[1024,1024]{1,0:T(8,128)} fusion(f32[2,1024,1024]{2,1,0:T(8,128)S(1)} %bitcast.66), kind=kLoop, calls=%fused_computation.49 | loop fusion | flops 1048576 | bytes 8388608 | tf_op jit(solution)/shard_map/neg | solution.py:48
  27.8 0.0 collective-permute-done
  27.8 18.2 %select_select_fusion = f32[2,1024,1024]{2,1,0:T(8,128)} fusion(f32[1024,1024]{1,0:T(8,128)S(1)} %get-tuple-element.22, pred[2]{0:T(512)(128)(4,1)S(1)} %get-tuple-element.25, pred[2]{0:T(512)(128)(4,1)S(1)} %get-tuple-element.26, f32[2,2,1,1024,512]{4,3,1,2,0:T(8,128)} %bitcast.70, f32[2,2,1,1024,512]{4,3,1,2,0:T(8,128)} %collective-permute-done, ...), kind=kOutput, calls=%fused_computation.17 | convolution fusion | flops 12894339072 | bytes 33555460 | tf_op jit(solution)/shard_map/sqin,nm->sqim/dot_general | solution.py:39
  46.0 10.2 %pad_maximum_fusion = f32[3,1024,1024]{2,1,0:T(8,128)} fusion(f32[1,1024,1024]{2,1,0:T(8,128)S(1)} %fusion.37, f32[2,1024,1024]{2,1,0:T(8,128)} %select_select_fusion), kind=kLoop, calls=%fused_computation.2 | loop fusion | flops 3145728 | bytes 25165824 | tf_op jit(solution)/shard_map/concatenate | solution.py:50
  56.2 19.3 %select_bitcast_fusion = f32[2,1,1024,1024]{3,2,0,1:T(8,128)} fusion(f32[1024,1024]{1,0:T(8,128)} %fusion.43, pred[2]{0:T(512)(128)(4,1)S(1)} %get-tuple-element.25, pred[2]{0:T(512)(128)(4,1)S(1)} %get-tuple-element.26, s32[]{:T(128)S(6)} %select_n.81, f32[1024,1024]{1,0:T(8,128)} %get-tuple-element.21, f32[2,2,1,1024,512]{4,3,1,2,0:T(8,128)} %collective-permute-done, ...), kind=kOutput, calls=%fused_computation.16 | convolution fusion | flops 12892241920 | bytes 33554440 | tf_op jit(solution)/shard_map/sqin,nm->sqim/dot_general | solution.py:39
  75.5 88.2 %all-reduce.4.cloned.1.call-done = (f32[1024,512]{1,0:T(8,128)}, f32[1024,512]{1,0:T(8,128)}, f32[1024,512]{1,0:T(8,128)}) async-done(((f32[1024,512]{1,0:T(8,128)}, f32[1024,512]{1,0:T(8,128)}, f32[1024,512]{1,0:T(8,128)}), (f32[1024,512]{1,0:T(8,128)}, f32[1024,512]{1,0:T(8,128)}, f32[1024,512]{1,0:T(8,128)})) %all-reduce.4.cloned.1.call-update) | async-done | bytes 6291472 | tf_op jit(solution)/shard_map/psum | solution.py:28
  163.6 1.0 collective-permute-start.1
  164.6 0.0 slice-start.2
  164.6 15.4 %fusion.30 = f32[3,1024,512]{2,1,0:T(8,128)} fusion(f32[3,1024,1024]{2,1,0:T(8,128)} %pad_maximum_fusion, f32[1024,512]{1,0:T(8,128)} %get-tuple-element.14), kind=kOutput, calls=%fused_computation.34 | convolution fusion | flops 9663676416 | bytes 20971520 | tf_op jit(solution)/shard_map/kim,mr->kir/dot_general | solution.py:56
  180.0 0.0 copy-start.2
  180.0 0.0 slice-start.3
  180.0 6.3 %add.37 = f32[3,1024,512]{2,1,0:T(8,128)S(1)} add(f32[3,1024,512]{2,1,0:T(8,128)} %concatenate.17, f32[3,1024,512]{2,1,0:T(8,128)} %fusion.30) | non-fusion elementwise | flops 1572864 | bytes 18874368 | tf_op jit(solution)/shard_map/add | solution.py:56
  186.4 0.0 copy-start.1
  186.4 0.0 collective-permute-done.1
  186.4 0.0 copy-done.2
  186.4 3.5 %fusion.15 = f32[1024,512]{1,0:T(8,128)S(1)} fusion(f32[1024,512]{1,0:T(8,128)S(1)} %collective-permute-done.1, f32[1024,512]{1,0:T(8,128)S(1)} %copy-done.2, f32[3,1024,512]{2,1,0:T(8,128)S(1)} %add.37), kind=kOutput, calls=%fused_computation.23 | convolution fusion | flops 3222274048 | bytes 8388608 | tf_op jit(solution)/shard_map/dot_general | solution.py:21
  190.0 0.0 copy-done.1
  190.0 0.5 sub.12
  190.4 0.0 slice-done.2
  190.5 0.0 slice-done.3
  190.5 8.8 %fusion.14 = f32[2,1,1024,512]{3,2,1,0:T(8,128)} fusion(f32[3,1024,512]{2,1,0:T(8,128)S(1)} %add.37, f32[1024,512]{1,0:T(8,128)S(1)} %sub.12, f32[2,1,1024,1024]{3,2,0,1:T(8,128)S(1)} %bitcast.68), kind=kOutput, calls=%fused_computation.22 | convolution fusion | flops 6443499520 | bytes 18874368 | tf_op jit(solution)/shard_map/sqim,mr->sqir/dot_general | solution.py:63
  (4 shorter events, 0.0 us)
Async XLA Ops:
  6.5 157.1 %all-reduce.4.cloned.1.call-start = ((), (), s32[]{:S(2)}) async-start(), calls=%async_computation | async-start | bytes 12582912 | tf_op jit(solution)/shard_map/psum | solution.py:28
  6.5 21.3 %collective-permute-start = (f32[2,2,1,1024,512]{4,3,1,2,0:T(8,128)}, f32[2,2,1,1024,512]{4,3,1,2,0:T(8,128)}, u32[]{:S(2)}, u32[]{:S(2)}) collective-permute-start(f32[2,2,1,1024,512]{4,3,1,2,0:T(8,128)} %bitcast.69), channel_id=1, source_target_pairs={{0,1},{1,0},{2,3},{3,2},{4,5},{5,4},{6,7},{7,6},{8,9},{9,8},{10,11... | collective-permute-start | bytes 25165832 | tf_op jit(solution)/shard_map/ppermute | solution.py:23
  8.0 3.3 %copy-start = (f32[2,1,1024,512]{3,2,1,0:T(8,128)S(1)}, f32[2,1,1024,512]{3,2,1,0:T(8,128)}, u32[]{:S(2)}) copy-start(f32[2,1,1024,512]{3,2,1,0:T(8,128)} %param.5) | copy-start | bytes 12582916
  13.8 6.3 %slice-start = ((s8[8388608]{0:T(1024)(128)(4,1)}), s8[4194304]{0:T(1024)(128)(4,1)S(1)}, s32[]{:S(2)}) async-start(s8[8388608]{0:T(1024)(128)(4,1)} %bitcast.65), calls=%async_computation.1 | async-start | bytes 8388608
  16.7 3.4 %slice-start.1 = ((s8[8388608]{0:T(1024)(128)(4,1)}), s8[4194304]{0:T(1024)(128)(4,1)S(1)}, s32[]{:S(2)}) async-start(s8[8388608]{0:T(1024)(128)(4,1)} %bitcast.65), calls=%async_computation.2 | async-start | bytes 8388608
  163.6 22.8 %collective-permute-start.1 = (f32[1024,512]{1,0:T(8,128)}, f32[1024,512]{1,0:T(8,128)S(1)}, u32[]{:S(2)}, u32[]{:S(2)}) collective-permute-start(f32[1024,512]{1,0:T(8,128)} %get-tuple-element.17), channel_id=1, source_target_pairs={{0,1},{1,0},{2,3},{3,2},{4,5},{5,4},{6,7},{7,6},{8,9},{9,8},{10,11... | collective-permute-start | bytes 6291464 | tf_op jit(solution)/shard_map/ppermute | solution.py:54
  164.6 25.8 %slice-start.2 = ((s8[8388608]{0:T(1024)(128)(4,1)}), s8[4194304]{0:T(1024)(128)(4,1)S(1)}, s32[]{:S(2)}) async-start(s8[8388608]{0:T(1024)(128)(4,1)} %bitcast.67), calls=%async_computation.3 | async-start | bytes 8388608
  180.0 6.4 %copy-start.2 = (f32[1024,512]{1,0:T(8,128)S(1)}, f32[1024,512]{1,0:T(8,128)}, u32[]{:S(2)}) copy-start(f32[1024,512]{1,0:T(8,128)} %get-tuple-element.17) | copy-start | bytes 6291460
  180.0 10.4 %slice-start.3 = ((s8[8388608]{0:T(1024)(128)(4,1)}), s8[4194304]{0:T(1024)(128)(4,1)S(1)}, s32[]{:S(2)}) async-start(s8[8388608]{0:T(1024)(128)(4,1)} %bitcast.67), calls=%async_computation.4 | async-start | bytes 8388608
  186.4 3.6 %copy-start.1 = (f32[1024,512]{1,0:T(8,128)S(1)}, f32[1024,512]{1,0:T(8,128)}, u32[]{:S(2)}) copy-start(f32[1024,512]{1,0:T(8,128)} %get-tuple-element.16) | copy-start | bytes 6291460
Sparse Core Ops, SparseCore 0:
  13.9 149.7 all-reduce.3

commit v3 on v1

--- a/solution.py
+++ b/solution.py
@@ -23,7 +23,7 @@
     other_panels = lax.ppermute(panels, "col", swap)
 
     def kept_at(owner, value):
-        return jnp.where(row_index == owner, value, 0).astype(value.dtype)
+        return value * (row_index == owner).astype(value.dtype)
 
     spread = lax.psum((kept_at(0, rhs[0, 0]), kept_at(1, rhs[0, 0]), kept_at(1, panels[0, 0, 0])), "row")
 

time: 200 us -> 200 us (level)
    mul x0 -> x2, other arithmetic: none -> 5.94 us  [kept_at(): return value * (row_index == owner).astype(value.dtype)]
    select_n x2 -> x0, other arithmetic: 5.94 us -> none  [kept_at(): return jnp.where(row_index == owner, value, 0).astype(value.dtype)]
where the time goes in v3:
time: 200 us
  waiting for transfers between devices  84.4 us (42%)
  matrix products  61.8 us (31%)
  other arithmetic  29.4 us (15%)
  between operations  13.5 us (7%)
  local copies, waits for them, and re-layouts  8.4 us (4%)
  starting transfers between devices  2.41 us (1%)
    psum x1, waiting for transfers between devices, per_device(): lax.psum((kept_at(0, rhs[0, 0]), kept_at(1, rhs[0, 0]), kept_at(1, panels...  84.4 us
    dot_general x2, matrix products, full_product(): jnp.einsum('sqin,nm->sqim', tiles, right, precision=high, preferred_eleme...  37.7 us
    dot_general x1, matrix products, per_device(): jnp.einsum('kim,mr->kir', first, rhs0, precision=high, preferred_element_...  13.5 us
    concatenate x1, other arithmetic, per_device(): jnp.concatenate([first.reshape((-1,) + first.shape[-2:]), inverse0[None]])  10.2 us
    dot_general x1, matrix products, per_device(): jnp.einsum(apply, second, sectioned1, precision=high, preferred_element_t...  7.12 us
    squeeze x1, local copies, waits for them, and re-layouts, per_device(): second = jnp.where(is_row0, zero, jnp.where(is_row1, -inverses[1], second))  6.67 us
    mul x2, other arithmetic, kept_at(): return value * (row_index == owner).astype(value.dtype)  5.94 us
    neg x1, other arithmetic, per_device(): second = jnp.where(is_row0, zero, jnp.where(is_row1, -inverses[1], second))  4.34 us
  transfers between devices with their start and end apart: 3, of which 1 were waited for; matrix products, arithmetic and copies ran while one was open for 42% of the time, Pallas kernels for 0%

profile of v3, /device:TPU:1, one launch (start us, length us, event | category | flops | bytes accessed | tf_op | source)
XLA Modules:
  0.0 200.0 jit_solution(7346642332969231812)
XLA Ops:
  6.5 0.0 all-reduce.3.cloned.1.call-start
  6.5 1.4 collective-permute-start
  8.0 0.0 copy-start.1
  8.0 3.3 %multiply_bitcast_fusion = f32[1024,512]{1,0:T(8,128)} fusion(f32[2,2,1,1024,512]{4,3,2,1,0:T(8,128)} %param.6, f32[]{:T(128)S(6)} %convert_element_type.10), kind=kLoop, calls=%fused_computation.37 | loop fusion | flops 524288 | bytes 4194308 | tf_op jit(solution)/shard_map/mul | solution.py:26
  11.3 0.0 copy-done.1
  11.3 2.6 %multiply_bitcast_fusion.1 = (f32[1024,512]{1,0:T(8,128)}, f32[1024,512]{1,0:T(8,128)}) fusion(f32[2,1,1024,512]{3,2,1,0:T(8,128)S(1)} %copy-done.1, f32[]{:T(128)S(6)} %convert_element_type.10, f32[]{:T(128)S(6)} %convert_element_type.9), kind=kLoop, calls=%fused_computation.38 | loop fusion | flops 1048576 | bytes 6291464 | tf_op jit(solution)/shard_map/mul | solution.py:26
  13.9 0.0 all-reduce.3.cloned.1.call-update
  14.0 6.7 %slice_bitcast_fusion.1 = (f32[1024,1024]{1,0:T(8,128)}, f32[1024,1024]{1,0:T(8,128)S(1)}) fusion(f32[2,1024,1024]{2,1,0:T(8,128)} %param.7), kind=kLoop, calls=%fused_computation.31 | loop fusion | bytes 16777216 | tf_op jit(solution)/shard_map/squeeze | solution.py:48
  20.7 0.0 copy-start.2
  20.7 0.0 slice-start
  20.7 2.0 fusion.34
  22.7 0.0 slice-start.1
  22.7 0.2 copy-done.2
  22.8 2.8 %bitcast_select_fusion = f32[2,1,1024,512]{3,2,0,1:T(8,128)} fusion(f32[2,1,1024,512]{3,2,1,0:T(8,128)S(1)} %copy-done.2, pred[2]{0:T(512)(128)(4,1)S(1)} %get-tuple-element.27), kind=kLoop, calls=%fused_computation.29 | loop fusion | flops 1048576 | bytes 8388610 | tf_op jit(solution)/shard_map/jit(_where)/select_n | solution.py:49
  25.7 0.0 slice-done
  25.7 1.5 slice-done.1
  27.2 4.3 %fusion.41 = (f32[1024,1024]{1,0:T(8,128)}, f32[1024,1024]{1,0:T(8,128)}) fusion(f32[2,1024,1024]{2,1,0:T(8,128)S(1)} %bitcast.68), kind=kLoop, calls=%fused_computation.51 | loop fusion | flops 2097152 | bytes 16777216 | tf_op jit(solution)/shard_map/neg | solution.py:48
  31.6 0.0 collective-permute-done
  31.6 18.4 %select_select_fusion = f32[2,1024,1024]{2,1,0:T(8,128)} fusion(f32[1024,1024]{1,0:T(8,128)} %get-tuple-element.24, pred[2]{0:T(512)(128)(4,1)S(1)} %get-tuple-element.28, pred[2]{0:T(512)(128)(4,1)S(1)} %broadcast_compare_fusion.2, f32[2,2,1,1024,512]{4,3,1,2,0:T(8,128)} %bitcast.70, f32[2,2,1,1024,512]{4,3,1,2,0:T(8,128)} %collective-permute-done, ...), kind=kOutput, calls=%fused_computation.17 | convolution fusion | flops 12892241920 | bytes 33554440 | tf_op jit(solution)/shard_map/sqin,nm->sqim/dot_general | solution.py:39
  50.0 10.2 %pad_maximum_fusion = f32[3,1024,1024]{2,1,0:T(8,128)} fusion(f32[1,1024,1024]{2,1,0:T(8,128)S(1)} %fusion.34, f32[2,1024,1024]{2,1,0:T(8,128)} %select_select_fusion), kind=kLoop, calls=%fused_computation.2 | loop fusion | flops 3145728 | bytes 25165824 | tf_op jit(solution)/shard_map/concatenate | solution.py:50
  60.2 19.3 %select_bitcast_fusion = f32[2,1,1024,1024]{3,2,0,1:T(8,128)} fusion(f32[1024,1024]{1,0:T(8,128)} %get-tuple-element.23, pred[2]{0:T(512)(128)(4,1)S(1)} %get-tuple-element.28, pred[2]{0:T(512)(128)(4,1)S(1)} %broadcast_compare_fusion.2, s32[]{:T(128)S(6)} %select_n.43, f32[1024,1024]{1,0:T(8,128)} %get-tuple-element.21, ...), kind=kOutput, calls=%fused_computation.16 | convolution fusion | flops 12892241920 | bytes 33554440 | tf_op jit(solution)/shard_map/sqin,nm->sqim/dot_general | solution.py:39
  79.4 84.4 %all-reduce.3.cloned.1.call-done = (f32[1024,512]{1,0:T(8,128)}, f32[1024,512]{1,0:T(8,128)}, f32[1024,512]{1,0:T(8,128)}) async-done(((f32[1024,512]{1,0:T(8,128)}, f32[1024,512]{1,0:T(8,128)}, f32[1024,512]{1,0:T(8,128)}), (f32[1024,512]{1,0:T(8,128)}, f32[1024,512]{1,0:T(8,128)}, f32[1024,512]{1,0:T(8,128)})) %all-reduce.3.cloned.1.call-update) | async-done | bytes 6291472 | tf_op jit(solution)/shard_map/psum | solution.py:28
  163.8 0.0 copy-start.5
  163.8 1.0 collective-permute-start.1
  164.8 13.5 %fusion.31 = f32[3,1024,512]{2,1,0:T(8,128)S(1)} fusion(f32[3,1024,1024]{2,1,0:T(8,128)} %pad_maximum_fusion, f32[1024,512]{1,0:T(8,128)} %get-tuple-element.14), kind=kOutput, calls=%fused_computation.35 | convolution fusion | flops 9663676416 | bytes 20971520 | tf_op jit(solution)/shard_map/kim,mr->kir/dot_general | solution.py:55
  178.3 0.0 copy-start.4
  178.3 0.0 collective-permute-done.1
  178.4 0.0 copy-done.5
  178.4 0.0 copy-start.3
  178.4 3.5 %fusion.17 = f32[1024,512]{1,0:T(8,128)S(1)} fusion(f32[1024,512]{1,0:T(8,128)S(1)} %collective-permute-done.1, f32[1024,512]{1,0:T(8,128)S(1)} %copy-done.5, f32[3,1024,512]{2,1,0:T(8,128)S(1)} %fusion.31), kind=kOutput, calls=%fused_computation.25 | convolution fusion | flops 3222274048 | bytes 8388608 | tf_op jit(solution)/shard_map/dot_general | solution.py:21
  181.9 0.0 copy-done.4
  181.9 0.5 sub.13
  182.4 0.0 copy-done.3
  182.4 0.0 copy-start
  182.4 7.1 %fusion.8 = f32[2,1024,512]{2,1,0:T(8,128)S(1)} fusion(f32[2,1,1024,1024]{3,2,0,1:T(8,128)S(1)} %copy-done.3, f32[1024,512]{1,0:T(8,128)S(1)} %sub.13), kind=kOutput, calls=%fused_computation.14 | convolution fusion | flops 6442450944 | bytes 14680064 | tf_op jit(solution)/shard_map/sqim,mr->sqir/dot_general | solution.py:62
  189.6 0.0 copy-done
  189.6 3.6 %fusion.16 = f32[2,1,1024,512]{3,2,1,0:T(8,128)} fusion(f32[2,1,1024,512]{3,2,0,1:T(8,128)S(1)} %copy-done, f32[3,1024,512]{2,1,0:T(8,128)S(1)} %fusion.31, f32[2,1024,512]{2,1,0:T(8,128)S(1)} %fusion.8), kind=kLoop, calls=%fused_computation.24 | loop fusion | flops 2097152 | bytes 16777216 | tf_op jit(solution)/shard_map/sub | solution.py:62
  (3 shorter events, 0.0 us)
Async XLA Ops:
  6.5 157.3 %all-reduce.3.cloned.1.call-start = ((), (), s32[]{:S(2)}) async-start(), calls=%async_computation | async-start | bytes 12582912 | tf_op jit(solution)/shard_map/psum | solution.py:28
  6.5 25.0 %collective-permute-start = (f32[2,2,1,1024,512]{4,3,1,2,0:T(8,128)}, f32[2,2,1,1024,512]{4,3,1,2,0:T(8,128)}, u32[]{:S(2)}, u32[]{:S(2)}) collective-permute-start(f32[2,2,1,1024,512]{4,3,1,2,0:T(8,128)} %bitcast.69), channel_id=1, source_target_pairs={{0,1},{1,0},{2,3},{3,2},{4,5},{5,4},{6,7},{7,6},{8,9},{9,8},{10,11... | collective-permute-start | bytes 25165832 | tf_op jit(solution)/shard_map/ppermute | solution.py:23
  8.0 3.3 %copy-start.1 = (f32[2,1,1024,512]{3,2,1,0:T(8,128)S(1)}, f32[2,1,1024,512]{3,2,1,0:T(8,128)}, u32[]{:S(2)}) copy-start(f32[2,1,1024,512]{3,2,1,0:T(8,128)} %param.5) | copy-start | bytes 12582916
  20.7 2.2 %copy-start.2 = (f32[2,1,1024,512]{3,2,1,0:T(8,128)S(1)}, f32[2,1,1024,512]{3,2,1,0:T(8,128)}, u32[]{:S(2)}) copy-start(f32[2,1,1024,512]{3,2,1,0:T(8,128)} %param.5) | copy-start | bytes 12582916
  20.7 5.0 %slice-start = ((s8[8388608]{0:T(1024)(128)(4,1)}), s8[4194304]{0:T(1024)(128)(4,1)S(1)}, s32[]{:S(2)}) async-start(s8[8388608]{0:T(1024)(128)(4,1)} %bitcast.67), calls=%async_computation.1 | async-start | bytes 8388608
  22.7 4.6 %slice-start.1 = ((s8[8388608]{0:T(1024)(128)(4,1)}), s8[4194304]{0:T(1024)(128)(4,1)S(1)}, s32[]{:S(2)}) async-start(s8[8388608]{0:T(1024)(128)(4,1)} %bitcast.67), calls=%async_computation.2 | async-start | bytes 8388608
  163.8 14.5 %copy-start.5 = (f32[1024,512]{1,0:T(8,128)S(1)}, f32[1024,512]{1,0:T(8,128)}, u32[]{:S(2)}) copy-start(f32[1024,512]{1,0:T(8,128)} %get-tuple-element.17) | copy-start | bytes 6291460
  163.8 14.5 %collective-permute-start.1 = (f32[1024,512]{1,0:T(8,128)}, f32[1024,512]{1,0:T(8,128)S(1)}, u32[]{:S(2)}, u32[]{:S(2)}) collective-permute-start(f32[1024,512]{1,0:T(8,128)} %get-tuple-element.17), channel_id=1, source_target_pairs={{0,1},{1,0},{2,3},{3,2},{4,5},{5,4},{6,7},{7,6},{8,9},{9,8},{10,11... | collective-permute-start | bytes 6291464 | tf_op jit(solution)/shard_map/ppermute | solution.py:53
  178.3 3.6 %copy-start.4 = (f32[1024,512]{1,0:T(8,128)S(1)}, f32[1024,512]{1,0:T(8,128)}, u32[]{:S(2)}) copy-start(f32[1024,512]{1,0:T(8,128)} %get-tuple-element.16) | copy-start | bytes 6291460
  178.4 4.1 %copy-start.3 = (f32[2,1,1024,1024]{3,2,0,1:T(8,128)S(1)}, f32[2,1,1024,1024]{3,2,0,1:T(8,128)}, u32[]{:S(2)}) copy-start(f32[2,1,1024,1024]{3,2,0,1:T(8,128)} %select_bitcast_fusion) | copy-start | bytes 25165828
  182.4 7.1 %copy-start = (f32[2,1,1024,512]{3,2,0,1:T(8,128)S(1)}, f32[2,1,1024,512]{3,2,0,1:T(8,128)}, u32[]{:S(2)}) copy-start(f32[2,1,1024,512]{3,2,0,1:T(8,128)} %bitcast_select_fusion) | copy-start | bytes 12582916
Sparse Core Ops, SparseCore 0:
  14.1 149.7 all-reduce.2

commit v4 on v3

--- a/solution.py
+++ b/solution.py
@@ -56,7 +56,6 @@
                         preferred_element_type=jnp.float32)
     solved0 = firsts[-1]
     sectioned1 = rhs1 - dot(jnp.concatenate([tile_mine, tile_other], axis=-1), solved0)
-    sectioned1 = lax.optimization_barrier(sectioned1)
     apply = "sqim,mr->sqir"
     out = kept - firsts[:-1].reshape(kept.shape)
     return out - jnp.einsum(apply, second, sectioned1, precision=high,

time: 200 us -> 200 us (level)
  no operation moved by 1% of the time
where the time goes in v4:
time: 200 us
  waiting for transfers between devices  84.4 us (42%)
  matrix products  62 us (31%)
  other arithmetic  28.9 us (14%)
  between operations  13.5 us (7%)
  local copies, waits for them, and re-layouts  8.39 us (4%)
  starting transfers between devices  2.41 us (1%)
    psum x1, waiting for transfers between devices, per_device(): lax.psum((kept_at(0, rhs[0, 0]), kept_at(1, rhs[0, 0]), kept_at(1, panels...  84.4 us
    dot_general x2, matrix products, full_product(): jnp.einsum('sqin,nm->sqim', tiles, right, precision=high, preferred_eleme...  37.7 us
    dot_general x1, matrix products, per_device(): jnp.einsum('kim,mr->kir', first, rhs0, precision=high, preferred_element_...  13.6 us
    concatenate x1, other arithmetic, per_device(): jnp.concatenate([first.reshape((-1,) + first.shape[-2:]), inverse0[None]])  10.2 us
    dot_general x1, matrix products, per_device(): jnp.einsum(apply, second, sectioned1, precision=high, preferred_element_t...  7.18 us
    squeeze x1, local copies, waits for them, and re-layouts, per_device(): second = jnp.where(is_row0, zero, jnp.where(is_row1, -inverses[1], second))  6.67 us
    mul x2, other arithmetic, kept_at(): return value * (row_index == owner).astype(value.dtype)  5.94 us
    neg x1, other arithmetic, per_device(): second = jnp.where(is_row0, zero, jnp.where(is_row1, -inverses[1], second))  4.34 us
  transfers between devices with their start and end apart: 3, of which 1 were waited for; matrix products, arithmetic and copies ran while one was open for 42% of the time, Pallas kernels for 0%

profile of v4, /device:TPU:1, one launch (start us, length us, event | category | flops | bytes accessed | tf_op | source)
XLA Modules:
  0.0 199.7 jit_solution(3777798044747675798)
XLA Ops:
  6.5 0.0 all-reduce.3.cloned.1.call-start
  6.5 1.4 collective-permute-start
  8.0 0.0 copy-start.1
  8.0 3.3 %multiply_bitcast_fusion = f32[1024,512]{1,0:T(8,128)} fusion(f32[2,2,1,1024,512]{4,3,2,1,0:T(8,128)} %param.6, f32[]{:T(128)S(6)} %convert_element_type.10), kind=kLoop, calls=%fused_computation.38 | loop fusion | flops 524288 | bytes 4194308 | tf_op jit(solution)/shard_map/mul | solution.py:26
  11.3 0.0 copy-done.1
  11.3 2.6 %multiply_bitcast_fusion.1 = (f32[1024,512]{1,0:T(8,128)}, f32[1024,512]{1,0:T(8,128)}) fusion(f32[2,1,1024,512]{3,2,1,0:T(8,128)S(1)} %copy-done.1, f32[]{:T(128)S(6)} %convert_element_type.10, f32[]{:T(128)S(6)} %convert_element_type.9), kind=kLoop, calls=%fused_computation.39 | loop fusion | flops 1048576 | bytes 6291464 | tf_op jit(solution)/shard_map/mul | solution.py:26
  13.9 0.0 all-reduce.3.cloned.1.call-update
  14.0 6.7 %slice_bitcast_fusion.1 = (f32[1024,1024]{1,0:T(8,128)}, f32[1024,1024]{1,0:T(8,128)S(1)}) fusion(f32[2,1024,1024]{2,1,0:T(8,128)} %param.7), kind=kLoop, calls=%fused_computation.31 | loop fusion | bytes 16777216 | tf_op jit(solution)/shard_map/squeeze | solution.py:48
  20.7 0.0 copy-start.2
  20.7 0.0 slice-start
  20.7 2.0 fusion.35
  22.7 0.0 slice-start.1
  22.7 0.2 copy-done.2
  22.8 2.8 %bitcast_select_fusion = f32[2,1,1024,512]{3,2,0,1:T(8,128)} fusion(f32[2,1,1024,512]{3,2,1,0:T(8,128)S(1)} %copy-done.2, pred[2]{0:T(512)(128)(4,1)S(1)} %get-tuple-element.27), kind=kLoop, calls=%fused_computation.29 | loop fusion | flops 1048576 | bytes 8388610 | tf_op jit(solution)/shard_map/jit(_where)/select_n | solution.py:49
  25.7 0.0 slice-done
  25.7 1.5 slice-done.1
  27.2 4.3 %fusion.42 = (f32[1024,1024]{1,0:T(8,128)}, f32[1024,1024]{1,0:T(8,128)}) fusion(f32[2,1024,1024]{2,1,0:T(8,128)S(1)} %bitcast.68), kind=kLoop, calls=%fused_computation.52 | loop fusion | flops 2097152 | bytes 16777216 | tf_op jit(solution)/shard_map/neg | solution.py:48
  31.6 0.0 collective-permute-done
  31.6 18.4 %select_select_fusion = f32[2,1024,1024]{2,1,0:T(8,128)} fusion(f32[1024,1024]{1,0:T(8,128)} %get-tuple-element.24, pred[2]{0:T(512)(128)(4,1)S(1)} %get-tuple-element.28, pred[2]{0:T(512)(128)(4,1)S(1)} %broadcast_compare_fusion.2, f32[2,2,1,1024,512]{4,3,1,2,0:T(8,128)} %bitcast.70, f32[2,2,1,1024,512]{4,3,1,2,0:T(8,128)} %collective-permute-done, ...), kind=kOutput, calls=%fused_computation.17 | convolution fusion | flops 12892241920 | bytes 33554440 | tf_op jit(solution)/shard_map/sqin,nm->sqim/dot_general | solution.py:39
  50.0 10.2 %pad_maximum_fusion = f32[3,1024,1024]{2,1,0:T(8,128)} fusion(f32[1,1024,1024]{2,1,0:T(8,128)S(1)} %fusion.35, f32[2,1024,1024]{2,1,0:T(8,128)} %select_select_fusion), kind=kLoop, calls=%fused_computation.2 | loop fusion | flops 3145728 | bytes 25165824 | tf_op jit(solution)/shard_map/concatenate | solution.py:50
  60.2 19.3 %select_bitcast_fusion = f32[2,1,1024,1024]{3,2,0,1:T(8,128)} fusion(f32[1024,1024]{1,0:T(8,128)} %get-tuple-element.23, pred[2]{0:T(512)(128)(4,1)S(1)} %get-tuple-element.28, pred[2]{0:T(512)(128)(4,1)S(1)} %broadcast_compare_fusion.2, s32[]{:T(128)S(6)} %select_n.43, f32[1024,1024]{1,0:T(8,128)} %get-tuple-element.21, ...), kind=kOutput, calls=%fused_computation.16 | convolution fusion | flops 12892241920 | bytes 33554440 | tf_op jit(solution)/shard_map/sqin,nm->sqim/dot_general | solution.py:39
  79.4 84.4 %all-reduce.3.cloned.1.call-done = (f32[1024,512]{1,0:T(8,128)}, f32[1024,512]{1,0:T(8,128)}, f32[1024,512]{1,0:T(8,128)}) async-done(((f32[1024,512]{1,0:T(8,128)}, f32[1024,512]{1,0:T(8,128)}, f32[1024,512]{1,0:T(8,128)}), (f32[1024,512]{1,0:T(8,128)}, f32[1024,512]{1,0:T(8,128)}, f32[1024,512]{1,0:T(8,128)})) %all-reduce.3.cloned.1.call-update) | async-done | bytes 6291472 | tf_op jit(solution)/shard_map/psum | solution.py:28
  163.8 0.0 copy-start.4
  163.8 1.0 collective-permute-start.1
  164.8 0.0 copy-start.5
  164.8 13.6 %fusion.31 = f32[3,1024,512]{2,1,0:T(8,128)S(1)} fusion(f32[3,1024,1024]{2,1,0:T(8,128)} %pad_maximum_fusion, f32[1024,512]{1,0:T(8,128)} %get-tuple-element.14), kind=kOutput, calls=%fused_computation.35 | convolution fusion | flops 9663676416 | bytes 20971520 | tf_op jit(solution)/shard_map/kim,mr->kir/dot_general | solution.py:55
  178.5 0.0 copy-start.3
  178.5 0.0 collective-permute-done.1
  178.5 0.0 copy-done.4
  178.5 3.5 %fusion.17 = f32[1024,512]{1,0:T(8,128)S(1)} fusion(f32[1024,512]{1,0:T(8,128)S(1)} %collective-permute-done.1, f32[1024,512]{1,0:T(8,128)S(1)} %copy-done.4, f32[3,1024,512]{2,1,0:T(8,128)S(1)} %fusion.31), kind=kOutput, calls=%fused_computation.25 | convolution fusion | flops 3222274048 | bytes 8388608 | tf_op jit(solution)/shard_map/dot_general | solution.py:21
  182.0 0.0 copy-done.5
  182.0 0.0 copy-done.3
  182.1 0.0 copy-start
  182.1 7.2 %fusion.8 = f32[2,1024,512]{2,1,0:T(8,128)S(1)} fusion(f32[2,1,1024,1024]{3,2,0,1:T(8,128)S(1)} %copy-done.3, f32[1024,512]{1,0:T(8,128)S(1)} %copy-done.5, f32[1024,512]{1,0:T(8,128)S(1)} %fusion.17), kind=kOutput, calls=%fused_computation.14 | convolution fusion | flops 6442975232 | bytes 16777216 | tf_op jit(solution)/shard_map/sqim,mr->sqir/dot_general | solution.py:61
  189.2 0.0 copy-done
  189.3 3.6 %fusion.16 = f32[2,1,1024,512]{3,2,1,0:T(8,128)} fusion(f32[2,1,1024,512]{3,2,0,1:T(8,128)S(1)} %copy-done, f32[3,1024,512]{2,1,0:T(8,128)S(1)} %fusion.31, f32[2,1024,512]{2,1,0:T(8,128)S(1)} %fusion.8), kind=kLoop, calls=%fused_computation.24 | loop fusion | flops 2097152 | bytes 16777216 | tf_op jit(solution)/shard_map/sub | solution.py:61
  (3 shorter events, 0.0 us)
Async XLA Ops:
  6.5 157.3 %all-reduce.3.cloned.1.call-start = ((), (), s32[]{:S(2)}) async-start(), calls=%async_computation | async-start | bytes 12582912 | tf_op jit(solution)/shard_map/psum | solution.py:28
  6.5 25.0 %collective-permute-start = (f32[2,2,1,1024,512]{4,3,1,2,0:T(8,128)}, f32[2,2,1,1024,512]{4,3,1,2,0:T(8,128)}, u32[]{:S(2)}, u32[]{:S(2)}) collective-permute-start(f32[2,2,1,1024,512]{4,3,1,2,0:T(8,128)} %bitcast.69), channel_id=1, source_target_pairs={{0,1},{1,0},{2,3},{3,2},{4,5},{5,4},{6,7},{7,6},{8,9},{9,8},{10,11... | collective-permute-start | bytes 25165832 | tf_op jit(solution)/shard_map/ppermute | solution.py:23
  8.0 3.3 %copy-start.1 = (f32[2,1,1024,512]{3,2,1,0:T(8,128)S(1)}, f32[2,1,1024,512]{3,2,1,0:T(8,128)}, u32[]{:S(2)}) copy-start(f32[2,1,1024,512]{3,2,1,0:T(8,128)} %param.5) | copy-start | bytes 12582916
  20.7 2.2 %copy-start.2 = (f32[2,1,1024,512]{3,2,1,0:T(8,128)S(1)}, f32[2,1,1024,512]{3,2,1,0:T(8,128)}, u32[]{:S(2)}) copy-start(f32[2,1,1024,512]{3,2,1,0:T(8,128)} %param.5) | copy-start | bytes 12582916
  20.7 5.0 %slice-start = ((s8[8388608]{0:T(1024)(128)(4,1)}), s8[4194304]{0:T(1024)(128)(4,1)S(1)}, s32[]{:S(2)}) async-start(s8[8388608]{0:T(1024)(128)(4,1)} %bitcast.67), calls=%async_computation.1 | async-start | bytes 8388608
  22.7 4.6 %slice-start.1 = ((s8[8388608]{0:T(1024)(128)(4,1)}), s8[4194304]{0:T(1024)(128)(4,1)S(1)}, s32[]{:S(2)}) async-start(s8[8388608]{0:T(1024)(128)(4,1)} %bitcast.67), calls=%async_computation.2 | async-start | bytes 8388608
  163.8 14.6 %copy-start.4 = (f32[1024,512]{1,0:T(8,128)S(1)}, f32[1024,512]{1,0:T(8,128)}, u32[]{:S(2)}) copy-start(f32[1024,512]{1,0:T(8,128)} %get-tuple-element.17) | copy-start | bytes 6291460
  163.8 14.6 %collective-permute-start.1 = (f32[1024,512]{1,0:T(8,128)}, f32[1024,512]{1,0:T(8,128)S(1)}, u32[]{:S(2)}, u32[]{:S(2)}) collective-permute-start(f32[1024,512]{1,0:T(8,128)} %get-tuple-element.17), channel_id=1, source_target_pairs={{0,1},{1,0},{2,3},{3,2},{4,5},{5,4},{6,7},{7,6},{8,9},{9,8},{10,11... | collective-permute-start | bytes 6291464 | tf_op jit(solution)/shard_map/ppermute | solution.py:53
  164.8 17.2 %copy-start.5 = (f32[1024,512]{1,0:T(8,128)S(1)}, f32[1024,512]{1,0:T(8,128)}, u32[]{:S(2)}) copy-start(f32[1024,512]{1,0:T(8,128)} %get-tuple-element.16) | copy-start | bytes 6291460
  178.5 3.6 %copy-start.3 = (f32[2,1,1024,1024]{3,2,0,1:T(8,128)S(1)}, f32[2,1,1024,1024]{3,2,0,1:T(8,128)}, u32[]{:S(2)}) copy-start(f32[2,1,1024,1024]{3,2,0,1:T(8,128)} %select_bitcast_fusion) | copy-start | bytes 25165828
  182.1 7.2 %copy-start = (f32[2,1,1024,512]{3,2,0,1:T(8,128)S(1)}, f32[2,1,1024,512]{3,2,0,1:T(8,128)}, u32[]{:S(2)}) copy-start(f32[2,1,1024,512]{3,2,0,1:T(8,128)} %bitcast_select_fusion) | copy-start | bytes 12582916
Sparse Core Ops, SparseCore 0:
  14.1 149.7 all-reduce.2
